TPU v7x, 32 devices: a whole 2x2x4 slice. The times are simulated.
32 devices in a mesh: ens: 2 (over y), step: 8 (over z, x), rows: 2 (over core).
Axes of the slice: x: 2, y: 2, z: 4, core: 2. Of those that a mesh axis runs over, the one named last changes fastest.
Arguments:
- iterates: float32 [8, 8, 32, 512], P('step', 'ens', 'rows'), parts along dimension 1, may hold values from -6 to 6
- window_start: float32 [8, 32, 512], P('ens', 'rows'), parts along dimension 0, may hold values from -6 to 6
- coarse: bfloat16 [24, 32, 512], P('ens', 'rows'), parts along dimension 0, may hold values from -6 to 6
- step_levels: int32 [8, 2], P('step'), may hold values from 0 to 16, as said below
- level_embed: bfloat16 [17, 128], replicated, may hold values from -3 to 3
- lift_weight: bfloat16 [16, 128], replicated, may hold values from -1.5 to 1.5
- conv_first: bfloat16 [3, 3, 128, 128], replicated, may hold values from -0.1875 to 0.1875
- conv_second: bfloat16 [3, 3, 128, 128], replicated, may hold values from -0.1875 to 0.1875
- project_weight: bfloat16 [128, 384], replicated, may hold values from -0.5 to 0.5
- mix_weight: bfloat16 [128, 128], replicated, may hold values from -6 to 6
- output_weight: bfloat16 [128, 4], replicated, may hold values from -0.5 to 0.5
Outputs:
- trajectory: float32 [8, 8, 32, 512], P('step', 'ens', 'rows'), parts along dimension 1
- denoised: float32 [8, 8, 32, 512], P('step', 'ens', 'rows'), parts along dimension 1
There are 2 independent parts, one for each index of `ens`. A program takes and returns all parts, laid end to end along the dimension named above; an argument that names none is the same for every part. Nothing has to cross between parts.
Inputs may be any that keep to these rules, and one draw needn't show every extreme that they name: `step_levels`: row k gives the plan levels at which step k starts and ends: each step ends 1 or 3 levels after it starts (half of the steps each), each step starts where the one before it ends, the first starts at level 0 and the last ends at level 16.
All inputs are finite; a program needn't handle non-finite values.
Results may differ from a plain program's by a relative error of at most 0.0028.
Values may be sent and summed in bfloat16 or wider, within the bound.
No kernel may reach another device: no remote copies, remote signals or barrier semaphores. Data moves between devices by JAX's collectives and lax.ppermute only.
A program may use at most 64 MiB of HBM per device.

v0:
```python
import jax
import jax.numpy as jnp
from jax import lax
from jax.sharding import PartitionSpec as P

HEAD_DIM = 64
SIGMA_TOP = 8.0
SIGMA_END = 0.002


def from_behind(x, axis, by):
    devices = lax.axis_size(axis)
    pairs = [(i, i + by) for i in range(devices) if 0 <= i + by < devices]
    return lax.ppermute(x, axis, pairs)


def with_halo(x, sides, width):
    for axis, dim in sides:
        devices, length = (lax.axis_size(axis), x.shape[dim])
        up = [(i, (i + 1) % devices) for i in range(devices - 1)]
        down = [(j, i) for i, j in up]
        last = lax.slice_in_dim(x, length - width, length, axis=dim)
        leading = lax.slice_in_dim(x, 0, width, axis=dim)
        before = lax.ppermute(last, axis, up)
        after = lax.ppermute(leading, axis, down)
        x = jnp.concatenate([before, x, after], axis=dim)
    return x


def noise_level(levels, level_count):
    fraction = levels.astype(jnp.float32) / jnp.float32(level_count - 1)
    return SIGMA_TOP * jnp.exp(fraction * jnp.log(jnp.float32(SIGMA_END / SIGMA_TOP)))


def normalize(values):
    return values * lax.rsqrt(jnp.mean(values * values, axis=-1, keepdims=True) + 1e-06)


def silu_norm(values):
    return jax.nn.silu(normalize(values)).astype(jnp.bfloat16)


def feature_map(values):
    return jnp.where(values > 0, values + 1.0, jnp.exp(jnp.minimum(values, 0.0)))


def conv_band(padded, weight):
    band_rows = padded.shape[0] - 2
    band_width = padded.shape[1]
    col_padded = jnp.pad(padded, ((0, 0), (1, 1), (0, 0)))
    stacked = jnp.concatenate(
        [
            col_padded[:, 0:band_width],
            col_padded[:, 1 : band_width + 1],
            col_padded[:, 2 : band_width + 2],
        ],
        axis=-1,
    )
    folded = weight.reshape(3, 3 * weight.shape[2], weight.shape[3])
    result = jnp.zeros((band_rows, band_width, weight.shape[3]), jnp.float32)
    for row_shift in range(3):
        result = result + jnp.einsum(
            "rwk,kf->rwf",
            stacked[row_shift : row_shift + band_rows],
            folded[row_shift],
            preferred_element_type=jnp.float32,
        )
    return result


def local(
    iterates,
    window_start,
    coarse,
    step_levels,
    level_embed,
    lift_weight,
    conv_first,
    conv_second,
    project_weight,
    mix_weight,
    output_weight,
):
    level_count = 2 * lax.axis_size("step") + 1
    previous = from_behind(iterates, "step", 1)
    current = jnp.where(lax.axis_index("step") == 0, window_start, previous[0])
    levels = step_levels[0]
    sigmas = noise_level(levels, level_count)
    sigma_low = sigmas[0]
    sigma_high = sigmas[1]
    spread = sigma_low * sigma_low + 0.25
    scale_in = lax.rsqrt(spread)
    scale_skip = 0.25 / spread
    scale_out = 0.5 * sigma_low * lax.rsqrt(spread)
    inputs = jnp.concatenate([(scale_in * current).astype(jnp.bfloat16), coarse], axis=0)
    picker = (jnp.arange(level_count) == levels[0]).astype(jnp.bfloat16)[None]
    embed_row = jnp.dot(picker, level_embed, preferred_element_type=jnp.float32)[0]
    lifted = (
        jnp.einsum("crw,cf->rwf", inputs, lift_weight, preferred_element_type=jnp.float32)
        + embed_row
    ).astype(jnp.bfloat16)
    band_rows = lifted.shape[0]
    band_width = lifted.shape[1]
    feat_dim = lifted.shape[2]
    act_first = silu_norm(lifted.astype(jnp.float32))
    padded = with_halo(act_first, (("rows", 0),), 1)
    middle = conv_band(padded, conv_first)
    act_next = silu_norm(middle)
    padded_next = with_halo(act_next, (("rows", 0),), 1)
    hidden = lifted.astype(jnp.float32) + conv_band(padded_next, conv_second)
    head_count = feat_dim // HEAD_DIM
    pooled = (
        hidden.reshape(band_rows // 4, 4, band_width // 4, 4, feat_dim)
        .mean(axis=(1, 3))
        .reshape(-1, feat_dim)
    )
    tokens = normalize(pooled).astype(jnp.bfloat16)
    projected = jnp.dot(tokens, project_weight, preferred_element_type=jnp.float32)
    queries = feature_map(projected[:, :feat_dim]).reshape(-1, head_count, HEAD_DIM)
    key_feats = feature_map(projected[:, feat_dim : 2 * feat_dim]).astype(jnp.bfloat16)
    value_rows = projected[:, 2 * feat_dim :].astype(jnp.bfloat16)
    key_piece = lax.all_gather(key_feats, "rows", axis=0, tiled=True)
    value_piece = lax.all_gather(value_rows, "rows", axis=0, tiled=True)
    piece_rows = key_piece.shape[0]
    key_heads = key_piece.reshape(piece_rows, head_count, HEAD_DIM)
    value_heads = value_piece.reshape(piece_rows, head_count, HEAD_DIM)
    summary_part = jnp.einsum(
        "thd,the->hde", key_heads, value_heads, preferred_element_type=jnp.float32
    )
    totals_part = jnp.sum(key_heads.astype(jnp.float32), axis=0)
    numerator = jnp.einsum("thd,hde->the", queries, summary_part, precision=lax.Precision.HIGHEST)
    denominator = jnp.einsum("thd,hd->th", queries, totals_part, precision=lax.Precision.HIGHEST)
    context = (numerator / denominator[:, :, None]).reshape(-1, feat_dim).astype(jnp.bfloat16)
    mixed = jnp.dot(context, mix_weight, preferred_element_type=jnp.float32)
    mixed = jnp.broadcast_to(
        mixed.reshape(band_rows // 4, 1, band_width // 4, 1, feat_dim),
        (band_rows // 4, 4, band_width // 4, 4, feat_dim),
    ).reshape(band_rows, band_width, feat_dim)
    act_out = silu_norm(hidden + mixed)
    out_field = jnp.einsum(
        "rwf,fc->crw", act_out, output_weight, preferred_element_type=jnp.float32
    )
    denoised = scale_skip * current + scale_out * out_field
    drift_step = (sigma_high - sigma_low) * (current - denoised) / sigma_low
    flattened = drift_step.reshape(1, -1)
    columns = lax.all_to_all(flattened, "step", split_axis=1, concat_axis=0, tiled=True)
    running = jnp.cumsum(columns, axis=0)
    summed = lax.all_to_all(running, "step", split_axis=0, concat_axis=1, tiled=True).reshape(
        drift_step.shape
    )
    trajectory = window_start + summed
    return (trajectory[None], denoised[None])


def solution(mesh):
    return jax.shard_map(
        local,
        mesh=mesh,
        in_specs=(
            P("step", "ens", "rows", None),
            P("ens", "rows", None),
            P("ens", "rows", None),
            P("step", None),
            P(),
            P(),
            P(),
            P(),
            P(),
            P(),
            P(),
        ),
        out_specs=(P("step", "ens", "rows", None), P("step", "ens", "rows", None)),
        check_vma=False,
    )
```

profile of v0, /device:TPU:0, one launch (start us, length us, event | category | flops | bytes accessed | tf_op | source)
XLA Modules:
  0.0 91.7 jit_solution(10086689503256885799)
XLA Ops:
  0.6 1.0 %copy.32 = f32[1,4,16,512]{3,1,2,0:T(4,128)S(1)} copy(f32[1,4,16,512]{3,2,1,0:T(8,128)} %param.11) | data formatting | bytes 262144 | tf_op args[0]
  1.7 4.8 %collective-permute-start = (f32[1,4,16,512]{3,1,2,0:T(4,128)S(1)}, f32[1,4,16,512]{3,1,2,0:T(4,128)S(1)}, u32[]{:S(2)}, u32[]{:S(2)}) collective-permute-start(f32[1,4,16,512]{3,1,2,0:T(4,128)S(1)} %copy.32), channel_id=1, source_target_pairs={{0,2},{2,4},{4,6},{6,8},{8,10},{10,12},{12,14},{1,3},{3,5},{5,7},{... | collective-permute-start | bytes 393224 | tf_op jit(solution)/shard_map/ppermute | solution.py:14
  6.5 0.7 exponential_multiply_fusion
  7.2 0.6 fusion.42
  9.2 1.0 %copy.34 = bf16[12,16,512]{2,0,1:T(8,128)(2,1)S(1)} copy(bf16[12,16,512]{2,1,0:T(8,128)(2,1)} %param.13) | data formatting | bytes 393216 | tf_op args[2]
  12.2 1.5 %convolution_bitcast_fusion.1 = f32[128]{0:T(128)S(1)} fusion(bf16[17,128]{1,0:T(8,128)(2,1)} %param.15, s32[]{:T(128)} %bitcast.110), kind=kOutput, calls=%fused_computation.34 | convolution fusion | flops 4369 | bytes 4868 | tf_op jit(solution)/shard_map/dot_general | solution.py:97
  13.6 1.0 %multiply_convert_fusion.7 = (bf16[4,16,512]{2,0,1:T(4,128)(2,1)S(1)}, f32[4,16,512]{2,0,1:T(4,128)S(1)}) fusion(f32[]{:T(128)S(6)} %rsqrt.37, f32[1,4,16,512]{3,1,2,0:T(4,128)S(1)} %collective-permute-done, f32[4,16,512]{2,1,0:T(8,128)} %param.12, pred[]{:T(512)S(6)} %eq.11), kind=kLoop, calls=%fused_computation.52 | loop fusion | flops 98304 | bytes 458757 | tf_op jit(solution)/shard_map/convert_element_type | solution.py:95
  14.7 2.6 %fusion.7 = (f32[16,512]{1,0:T(8,128)S(1)}, bf16[16,512,128]{2,1,0:T(8,128)(2,1)S(1)}) fusion(f32[128]{0:T(128)S(1)} %convolution_bitcast_fusion.1, bf16[16,128]{1,0:T(8,128)(2,1)} %param.16, bf16[12,16,512]{2,0,1:T(8,128)(2,1)S(1)} %copy.34, bf16[4,16,512]{2,0,1:T(4,128)(2,1)S(1)} %get-tuple-element.12), kind=kOutput, calls=%fused_computation.14 | convolution fusion | flops 39313408 | bytes 2396672 | tf_op jit(solution)/shard_map/crw,cf->rwf/dot_general | solution.py:99
  17.3 1.5 %fusion.6 = bf16[16,512,128]{2,1,0:T(8,128)(2,1)S(1)} fusion(bf16[16,512,128]{2,1,0:T(8,128)(2,1)S(1)} %get-tuple-element.35, f32[16,512]{1,0:T(8,128)S(1)} %add_rsqrt_fusion.2), kind=kLoop, calls=%fused_computation.13 | loop fusion | flops 7340032 | bytes 4227072 | tf_op jit(solution)/shard_map/convert_element_type | solution.py:40
  18.8 1.5 %collective-permute-start.1 = (bf16[1,512,128]{2,1,0:T(8,128)(2,1)S(1)}, bf16[1,512,128]{2,1,0:T(8,128)(2,1)S(1)}, u32[]{:S(2)}, u32[]{:S(2)}) collective-permute-start(bf16[1,512,128]{2,1,0:T(8,128)(2,1)S(1)} %get-tuple-element.20), channel_id=1, source_target_pairs={{0,1},{2,3},{4,5},{6,7},{8,9},{10,11},{12,13},{14,15},{16,17},{18,... | collective-permute-start | bytes 393224 | tf_op jit(solution)/shard_map/ppermute | solution.py:24
  20.3 1.3 %collective-permute-start.2 = (bf16[1,512,128]{2,1,0:T(8,128)(2,1)S(1)}, bf16[1,512,128]{2,1,0:T(8,128)(2,1)S(1)}, u32[]{:S(2)}, u32[]{:S(2)}) collective-permute-start(bf16[1,512,128]{2,1,0:T(8,128)(2,1)S(1)} %get-tuple-element.21), channel_id=1, source_target_pairs={{1,0},{3,2},{5,4},{7,6},{9,8},{11,10},{13,12},{15,14},{17,16},{19,... | collective-permute-start | bytes 393224 | tf_op jit(solution)/shard_map/ppermute | solution.py:25
  21.7 1.9 %collective-permute-done.2 = bf16[1,512,128]{2,1,0:T(8,128)(2,1)S(1)} collective-permute-done((bf16[1,512,128]{2,1,0:T(8,128)(2,1)S(1)}, bf16[1,512,128]{2,1,0:T(8,128)(2,1)S(1)}, u32[]{:S(2)}, u32[]{:S(2)}) %collective-permute-start.2) | collective-permute-done | bytes 131104 | tf_op jit(solution)/shard_map/ppermute | solution.py:25
  23.6 1.4 %fusion.12 = bf16[18,514,128]{2,1,0:T(8,128)(2,1)S(1)} fusion(bf16[1,512,128]{2,1,0:T(8,128)(2,1)S(1)} %collective-permute-done.2, bf16[16,512,128]{2,1,0:T(8,128)(2,1)S(1)} %fusion.6, bf16[1,512,128]{2,1,0:T(8,128)(2,1)S(1)} %collective-permute-done.1), kind=kLoop, calls=%fused_computation.27 | loop fusion | flops 14211072 | bytes 4727808 | tf_op jit(solution)/shard_map/concatenate | solution.py:26
  25.0 1.4 %fusion.37 = (bf16[18,512,128]{2,1,0:T(8,128)(2,1)S(1)}, bf16[18,512,128]{2,1,0:T(8,128)(2,1)S(1)}) fusion(bf16[18,514,128]{2,1,0:T(8,128)(2,1)S(1)} %fusion.12), kind=kLoop, calls=%fused_computation.71 | loop fusion | bytes 9437184 | tf_op jit(solution)/shard_map/slice | solution.py:53
  26.5 1.1 %pad_maximum_fusion = bf16[18,512,384]{2,1,0:T(8,128)(2,1)S(1)} fusion(bf16[18,512,128]{2,1,0:T(8,128)(2,1)S(1)} %get-tuple-element.17, bf16[1,512,128]{2,1,0:T(8,128)(2,1)S(1)} %collective-permute-done.2, bf16[16,512,128]{2,1,0:T(8,128)(2,1)S(1)} %fusion.6, bf16[1,512,128]{2,1,0:T(8,128)(2,1)S(1)} %collective-permute-done.1, ...), kind=kLoop, calls=%fused_computation.2 | loop fusion | flops 35389440 | bytes 14155776 | tf_op jit(solution)/shard_map/concatenate | solution.py:51
  27.6 1.8 %fusion.46 = f32[16,512,128]{2,1,0:T(8,128)S(1)} fusion(bf16[18,512,384]{2,1,0:T(8,128)(2,1)S(1)} %pad_maximum_fusion, bf16[384,128,1]{1,0,2:T(8,128)(2,1)S(1)} %bitcast.106), kind=kOutput, calls=%fused_computation.80 | convolution fusion | flops 805306368 | bytes 11370496 | tf_op jit(solution)/shard_map/rwk,kf->rwf/dot_general | solution.py:62
  29.4 1.8 %fusion.47 = f32[16,512,128]{2,1,0:T(8,128)S(1)} fusion(bf16[18,512,384]{2,1,0:T(8,128)(2,1)S(1)} %pad_maximum_fusion, bf16[384,128,1]{1,0,2:T(8,128)(2,1)S(1)} %bitcast.104), kind=kOutput, calls=%fused_computation.81 | convolution fusion | flops 805306368 | bytes 11370496 | tf_op jit(solution)/shard_map/rwk,kf->rwf/dot_general | solution.py:62
  31.2 2.1 %multiply_reduce_fusion.1 = (f32[16,512]{1,0:T(8,128)S(1)}, f32[16,512,128]{2,1,0:T(8,128)S(1)}) fusion(bf16[18,512,384]{2,1,0:T(8,128)(2,1)S(1)} %pad_maximum_fusion, bf16[384,128,1]{1,0,2:T(8,128)(2,1)S(1)} %bitcast.102, f32[16,512,128]{2,1,0:T(8,128)S(1)} %fusion.46, f32[16,512,128]{2,1,0:T(8,128)S(1)} %fusion.47), kind=kOutput, calls=%fused_computation.18 | convolution fusion | flops 809492480 | bytes 19791872 | tf_op jit(solution)/shard_map/rwk,kf->rwf/dot_general | solution.py:62
  33.3 1.4 %multiply_convert_fusion.1 = bf16[16,512,128]{2,1,0:T(8,128)(2,1)S(1)} fusion(f32[16,512,128]{2,1,0:T(8,128)S(1)} %get-tuple-element.37, f32[16,512]{1,0:T(8,128)S(1)} %add_rsqrt_fusion.1), kind=kLoop, calls=%fused_computation.17 | loop fusion | flops 6291456 | bytes 6324224 | tf_op jit(solution)/shard_map/convert_element_type | solution.py:40
  34.8 2.1 %collective-permute-start.3 = (bf16[1,512,128]{2,1,0:T(8,128)(2,1)S(1)}, bf16[1,512,128]{2,1,0:T(8,128)(2,1)S(1)}, u32[]{:S(2)}, u32[]{:S(2)}) collective-permute-start(bf16[1,512,128]{2,1,0:T(8,128)(2,1)S(1)} %get-tuple-element.18), channel_id=1, source_target_pairs={{0,1},{2,3},{4,5},{6,7},{8,9},{10,11},{12,13},{14,15},{16,17},{18,... | collective-permute-start | bytes 393224 | tf_op jit(solution)/shard_map/ppermute | solution.py:24
  36.9 1.5 %collective-permute-start.4 = (bf16[1,512,128]{2,1,0:T(8,128)(2,1)S(1)}, bf16[1,512,128]{2,1,0:T(8,128)(2,1)S(1)}, u32[]{:S(2)}, u32[]{:S(2)}) collective-permute-start(bf16[1,512,128]{2,1,0:T(8,128)(2,1)S(1)} %get-tuple-element.19), channel_id=1, source_target_pairs={{1,0},{3,2},{5,4},{7,6},{9,8},{11,10},{13,12},{15,14},{17,16},{19,... | collective-permute-start | bytes 393224 | tf_op jit(solution)/shard_map/ppermute | solution.py:25
  38.4 1.7 %collective-permute-done.4 = bf16[1,512,128]{2,1,0:T(8,128)(2,1)S(1)} collective-permute-done((bf16[1,512,128]{2,1,0:T(8,128)(2,1)S(1)}, bf16[1,512,128]{2,1,0:T(8,128)(2,1)S(1)}, u32[]{:S(2)}, u32[]{:S(2)}) %collective-permute-start.4) | collective-permute-done | bytes 131104 | tf_op jit(solution)/shard_map/ppermute | solution.py:25
  40.1 1.4 %select_maximum_fusion = bf16[18,514,128]{2,1,0:T(8,128)(2,1)S(1)} fusion(bf16[1,512,128]{2,1,0:T(8,128)(2,1)S(1)} %collective-permute-done.4, bf16[16,512,128]{2,1,0:T(8,128)(2,1)S(1)} %multiply_convert_fusion.1, bf16[1,512,128]{2,1,0:T(8,128)(2,1)S(1)} %collective-permute-done.3), kind=kLoop, calls=%fused_computation.21 | loop fusion | flops 14211072 | bytes 4727808 | tf_op jit(solution)/shard_map/concatenate | solution.py:26
  41.5 1.5 %fusion.36 = (bf16[18,512,128]{2,1,0:T(8,128)(2,1)S(1)}, bf16[18,512,128]{2,1,0:T(8,128)(2,1)S(1)}) fusion(bf16[18,514,128]{2,1,0:T(8,128)(2,1)S(1)} %select_maximum_fusion), kind=kLoop, calls=%fused_computation.70 | loop fusion | bytes 9437184 | tf_op jit(solution)/shard_map/slice | solution.py:53
  43.0 1.1 %pad_maximum_fusion.1 = bf16[18,512,384]{2,1,0:T(8,128)(2,1)S(1)} fusion(bf16[18,512,128]{2,1,0:T(8,128)(2,1)S(1)} %get-tuple-element.15, bf16[1,512,128]{2,1,0:T(8,128)(2,1)S(1)} %collective-permute-done.4, bf16[16,512,128]{2,1,0:T(8,128)(2,1)S(1)} %multiply_convert_fusion.1, bf16[1,512,128]{2,1,0:T(8,128)(2,1)S(1)} %collective-permute-done.3, ...), kind=kLoop, calls=%fused_computation.3 | loop fusion | flops 35389440 | bytes 14155776 | tf_op jit(solution)/shard_map/concatenate | solution.py:51
  44.2 1.8 %fusion.48 = f32[16,512,128]{2,1,0:T(8,128)S(1)} fusion(bf16[18,512,384]{2,1,0:T(8,128)(2,1)S(1)} %pad_maximum_fusion.1, bf16[384,128,1]{1,0,2:T(8,128)(2,1)S(1)} %bitcast.107), kind=kOutput, calls=%fused_computation.82 | convolution fusion | flops 805306368 | bytes 11370496 | tf_op jit(solution)/shard_map/rwk,kf->rwf/dot_general | solution.py:62
  46.0 1.8 %fusion.49 = f32[16,512,128]{2,1,0:T(8,128)S(1)} fusion(bf16[18,512,384]{2,1,0:T(8,128)(2,1)S(1)} %pad_maximum_fusion.1, bf16[384,128,1]{1,0,2:T(8,128)(2,1)S(1)} %bitcast.105), kind=kOutput, calls=%fused_computation.83 | convolution fusion | flops 805306368 | bytes 11370496 | tf_op jit(solution)/shard_map/rwk,kf->rwf/dot_general | solution.py:62
  47.8 3.9 %convert_add_fusion = f32[16,512,128]{2,1,0:T(8,128)} fusion(bf16[16,512,128]{2,1,0:T(8,128)(2,1)S(1)} %get-tuple-element.35, f32[16,512,128]{2,1,0:T(8,128)S(1)} %fusion.48, f32[16,512,128]{2,1,0:T(8,128)S(1)} %fusion.49, bf16[18,512,384]{2,1,0:T(8,128)(2,1)S(1)} %pad_maximum_fusion.1, bf16[384,128,1]{1,0,2:T(8,128)(2,1)S(1)} %bitcast.103), kind=kOutput, calls=%fused_computation.4 | convolution fusion | flops 809500672 | bytes 21856256 | tf_op jit(solution)/shard_map/rwk,kf->rwf/dot_general | solution.py:62
  51.7 3.2 %reduce_sum.60 = f32[4,128,128]{2,1,0:T(8,128)S(1)} reduce(f32[4,4,128,4,128]{4,3,2,1,0:T(4,128)} %bitcast.96, f32[]{:T(128)} %constant.40.clone.1), dimensions={1,3}, to_apply=%region_2.3 | reduce | flops 983040 | bytes 4456452 | tf_op jit(solution)/shard_map/reduce_sum | solution.py:114
  55.2 0.3 fusion.43
  55.7 2.0 %all_gather.6 = bf16[1024,128]{0,1:T(8,128)(2,1)S(1)} all-gather(bf16[512,128]{0,1:T(8,128)(2,1)S(1)} %get-tuple-element.23), channel_id=1, replica_groups=mesh['ens'=2,'step'=8,'rows'=2] {'rows'}, dimensions={0}, use_global_device_ids=true | all-gather | bytes 393216 | tf_op jit(solution)/shard_map/all_gather | solution.py:122
  57.8 0.2 fusion.45
  58.1 2.2 %all_gather.7 = bf16[1024,128]{0,1:T(8,128)(2,1)S(1)} all-gather(bf16[512,128]{0,1:T(8,128)(2,1)S(1)} %slice.130), channel_id=1, replica_groups=mesh['ens'=2,'step'=8,'rows'=2] {'rows'}, dimensions={0}, use_global_device_ids=true | all-gather | bytes 393216 | tf_op jit(solution)/shard_map/all_gather | solution.py:123
  60.3 0.2 fusion.44
  60.6 0.4 fusion.15
  61.0 0.2 fusion.24
  61.2 0.8 broadcast_in_dim.6
  62.0 1.1 %copy-done.1 = f32[16,512,128]{2,1,0:T(8,128)S(1)} copy-done((f32[16,512,128]{2,1,0:T(8,128)S(1)}, f32[16,512,128]{2,1,0:T(8,128)}, u32[]{:S(2)}) %copy-start.1) | copy-done | bytes 4194328
  63.2 1.2 %multiply_reduce_fusion = (f32[16,512]{1,0:T(8,128)S(1)}, f32[16,512,128]{2,1,0:T(8,128)S(1)}) fusion(f32[16,512,128]{2,1,0:T(8,128)S(1)} %copy-done.1, f32[16,512,128]{2,1,0:T(8,128)S(1)} %bitcast.97), kind=kLoop, calls=%fused_computation.16 | loop fusion | flops 3137536 | bytes 12615680 | tf_op jit(solution)/shard_map/reduce_sum | solution.py:36
  64.4 1.9 %fusion.17 = f32[4,16,512]{2,0,1:T(4,128)S(1)} fusion(f32[16,512,128]{2,1,0:T(8,128)S(1)} %get-tuple-element.11, f32[16,512]{1,0:T(8,128)S(1)} %add_rsqrt_fusion, f32[]{:T(128)S(6)} %mul.111, bf16[128,4]{0,1:T(4,128)(2,1)S(1)} %copy-done.6), kind=kOutput, calls=%fused_computation.33 | convolution fusion | flops 14712832 | bytes 4359172 | tf_op jit(solution)/shard_map/rwf,fc->crw/dot_general | solution.py:140
  66.3 0.7 fusion.26
  67.2 12.0 %all_to_all.24 = f32[1,8,4096]{2,0,1:T(1,128)S(1)} all-to-all(f32[1,8,4096]{2,0,1:T(1,128)S(1)} %all_to_all.21), channel_id=1, replica_groups=mesh['ens'=2,'step'=8,'rows'=2] {'step'}, dimensions={1} | all-to-all | bytes 262144 | tf_op jit(solution)/shard_map/all_to_all | solution.py:146
  79.2 0.7 fusion.22
  80.0 3.4 %all-to-all-start.1 = ((f32[8,1,4096]{2,1,0:T(1,128)}), f32[8,1,4096]{2,1,0:T(1,128)S(1)}, u32[]{:S(2)}, u32[]{:S(2)}) async-start(f32[8,1,4096]{2,1,0:T(1,128)} %fusion.22), calls=%async_computation.1 | async-start | bytes 262144 | tf_op jit(solution)/shard_map/all_to_all | solution.py:148
  83.4 0.7 copy.39
  84.0 6.6 %all-to-all-done.1 = f32[8,1,4096]{2,1,0:T(1,128)S(1)} async-done(((f32[8,1,4096]{2,1,0:T(1,128)}), f32[8,1,4096]{2,1,0:T(1,128)S(1)}, u32[]{:S(2)}, u32[]{:S(2)}) %all-to-all-start.1) | async-done | bytes 131104 | tf_op jit(solution)/shard_map/all_to_all | solution.py:148
  90.6 0.3 reduce.2
  91.0 0.7 add_bitcast_fusion
  (35 shorter events, 1.1 us)
Async XLA Ops:
  0.6 54.6 %copy-start = (bf16[128,384]{1,0:T(8,128)(2,1)S(1)}, bf16[128,384]{1,0:T(8,128)(2,1)}, u32[]{:S(2)}) copy-start(bf16[128,384]{1,0:T(8,128)(2,1)} %param.19) | copy-start | bytes 294916
  1.7 12.0 %collective-permute-start = (f32[1,4,16,512]{3,1,2,0:T(4,128)S(1)}, f32[1,4,16,512]{3,1,2,0:T(4,128)S(1)}, u32[]{:S(2)}, u32[]{:S(2)}) collective-permute-start(f32[1,4,16,512]{3,1,2,0:T(4,128)S(1)} %copy.32), channel_id=1, source_target_pairs={{0,2},{2,4},{4,6},{6,8},{8,10},{10,12},{12,14},{1,3},{3,5},{5,7},{... | collective-permute-start | bytes 393224 | tf_op jit(solution)/shard_map/ppermute | solution.py:14
  14.7 7.0 %copy-start.3 = (bf16[3,3,128,128]{3,2,1,0:T(8,128)(2,1)S(1)}, bf16[3,3,128,128]{3,2,1,0:T(8,128)(2,1)}, u32[]{:S(2)}) copy-start(bf16[3,3,128,128]{3,2,1,0:T(8,128)(2,1)} %param.17) | copy-start | bytes 884740
  18.8 2.8 %collective-permute-start.1 = (bf16[1,512,128]{2,1,0:T(8,128)(2,1)S(1)}, bf16[1,512,128]{2,1,0:T(8,128)(2,1)S(1)}, u32[]{:S(2)}, u32[]{:S(2)}) collective-permute-start(bf16[1,512,128]{2,1,0:T(8,128)(2,1)S(1)} %get-tuple-element.20), channel_id=1, source_target_pairs={{0,1},{2,3},{4,5},{6,7},{8,9},{10,11},{12,13},{14,15},{16,17},{18,... | collective-permute-start | bytes 393224 | tf_op jit(solution)/shard_map/ppermute | solution.py:24
  20.3 3.2 %collective-permute-start.2 = (bf16[1,512,128]{2,1,0:T(8,128)(2,1)S(1)}, bf16[1,512,128]{2,1,0:T(8,128)(2,1)S(1)}, u32[]{:S(2)}, u32[]{:S(2)}) collective-permute-start(bf16[1,512,128]{2,1,0:T(8,128)(2,1)S(1)} %get-tuple-element.21), channel_id=1, source_target_pairs={{1,0},{3,2},{5,4},{7,6},{9,8},{11,10},{13,12},{15,14},{17,16},{19,... | collective-permute-start | bytes 393224 | tf_op jit(solution)/shard_map/ppermute | solution.py:25
  33.3 5.1 %copy-start.4 = (bf16[3,3,128,128]{3,2,1,0:T(8,128)(2,1)S(1)}, bf16[3,3,128,128]{3,2,1,0:T(8,128)(2,1)}, u32[]{:S(2)}) copy-start(bf16[3,3,128,128]{3,2,1,0:T(8,128)(2,1)} %param.18) | copy-start | bytes 884740
  34.8 3.6 %collective-permute-start.3 = (bf16[1,512,128]{2,1,0:T(8,128)(2,1)S(1)}, bf16[1,512,128]{2,1,0:T(8,128)(2,1)S(1)}, u32[]{:S(2)}, u32[]{:S(2)}) collective-permute-start(bf16[1,512,128]{2,1,0:T(8,128)(2,1)S(1)} %get-tuple-element.18), channel_id=1, source_target_pairs={{0,1},{2,3},{4,5},{6,7},{8,9},{10,11},{12,13},{14,15},{16,17},{18,... | collective-permute-start | bytes 393224 | tf_op jit(solution)/shard_map/ppermute | solution.py:24
  36.9 3.2 %collective-permute-start.4 = (bf16[1,512,128]{2,1,0:T(8,128)(2,1)S(1)}, bf16[1,512,128]{2,1,0:T(8,128)(2,1)S(1)}, u32[]{:S(2)}, u32[]{:S(2)}) collective-permute-start(bf16[1,512,128]{2,1,0:T(8,128)(2,1)S(1)} %get-tuple-element.19), channel_id=1, source_target_pairs={{1,0},{3,2},{5,4},{7,6},{9,8},{11,10},{13,12},{15,14},{17,16},{19,... | collective-permute-start | bytes 393224 | tf_op jit(solution)/shard_map/ppermute | solution.py:25
  51.7 9.3 %copy-start.5 = (bf16[128,128]{1,0:T(8,128)(2,1)S(1)}, bf16[128,128]{1,0:T(8,128)(2,1)}, u32[]{:S(2)}) copy-start(bf16[128,128]{1,0:T(8,128)(2,1)} %param.20) | copy-start | bytes 98308
  61.0 2.2 %copy-start.1 = (f32[16,512,128]{2,1,0:T(8,128)S(1)}, f32[16,512,128]{2,1,0:T(8,128)}, u32[]{:S(2)}) copy-start(f32[16,512,128]{2,1,0:T(8,128)} %convert_add_fusion) | copy-start | bytes 12582916
  63.2 1.2 %copy-start.6 = (bf16[128,4]{0,1:T(4,128)(2,1)S(1)}, bf16[128,4]{0,1:T(4,128)(2,1)}, u32[]{:S(2)}) copy-start(bf16[128,4]{0,1:T(4,128)(2,1)} %param.21) | copy-start | bytes 3076
  64.4 26.6 %copy-start.2 = (f32[4,16,512]{2,1,0:T(8,128)S(1)}, f32[4,16,512]{2,1,0:T(8,128)}, u32[]{:S(2)}) copy-start(f32[4,16,512]{2,1,0:T(8,128)} %param.12) | copy-start | bytes 393220
  80.0 10.7 %all-to-all-start.1 = ((f32[8,1,4096]{2,1,0:T(1,128)}), f32[8,1,4096]{2,1,0:T(1,128)S(1)}, u32[]{:S(2)}, u32[]{:S(2)}) async-start(f32[8,1,4096]{2,1,0:T(1,128)} %fusion.22), calls=%async_computation.1 | async-start | bytes 262144 | tf_op jit(solution)/shard_map/all_to_all | solution.py:148
where the time goes:
time: 92.3 us; the launch traced here: 91.7 us
  matrix products  20.5 us (22%)
  other arithmetic  17.1 us (19%)
  blocking collectives  16.2 us (18%)
  starting transfers between devices  14.5 us (16%)
  waiting for transfers between devices  10.2 us (11%)
  local copies, waits for them, and re-layouts  8.69 us (9%)
  between operations  4.39 us (5%)
    dot_general x6, matrix products, conv_band(): jnp.einsum('rwk,kf->rwf', stacked[row_shift:row_shift + band_rows], folde...  13.1 us
    all_to_all x1, blocking collectives, local(): lax.all_to_all(flattened, 'step', split_axis=1, concat_axis=0, tiled=True)  12 us
    all_to_all x1, waiting for transfers between devices, local(): lax.all_to_all(running, 'step', split_axis=0, concat_axis=1, tiled=True)  6.58 us
    ppermute x1, starting transfers between devices, from_behind(): return lax.ppermute(x, axis, pairs)  4.85 us
    unnamed x17, local copies, waits for them, and re-layouts  3.94 us
    ppermute x2, waiting for transfers between devices, with_halo(): after = lax.ppermute(leading, axis, down)  3.6 us
    ppermute x2, starting transfers between devices, with_halo(): before = lax.ppermute(last, axis, up)  3.53 us
    all_to_all x1, starting transfers between devices, local(): lax.all_to_all(running, 'step', split_axis=0, concat_axis=1, tiled=True)  3.37 us
  transfers between devices with their start and end apart: 6, of which 3 were waited for; matrix products, arithmetic and copies ran while one was open for 5% of the time, Pallas kernels for 0%

commit v1 on v0

--- a/solution.py
+++ b/solution.py
@@ -119,7 +119,9 @@
     queries = feature_map(projected[:, :feat_dim]).reshape(-1, head_count, HEAD_DIM)
     key_feats = feature_map(projected[:, feat_dim : 2 * feat_dim]).astype(jnp.bfloat16)
     value_rows = projected[:, 2 * feat_dim :].astype(jnp.bfloat16)
-    key_piece = lax.all_gather(key_feats, "rows", axis=0, tiled=True)
+    key_piece = jnp.concatenate(
+        lax.all_to_all(jnp.stack([key_feats] * lax.axis_size("rows")), "rows", 0, 0), axis=0
+    )
     value_piece = lax.all_gather(value_rows, "rows", axis=0, tiled=True)
     piece_rows = key_piece.shape[0]
     key_heads = key_piece.reshape(piece_rows, head_count, HEAD_DIM)

time: 92.3 us -> 94.8 us (1.027)
  blocking collectives: 16.2 us -> 18.2 us
    all_to_all x0 -> x1, blocking collectives: none -> 3.94 us  [local(): lax.all_to_all(jnp.stack([key_feats] * lax.axis_size('rows')), 'rows', 0, 0)]
    all_gather x1 -> x0, blocking collectives: 1.99 us -> none  [local(): key_piece = lax.all_gather(key_feats, 'rows', axis=0, tiled=True)]
where the time goes in v1:
time: 94.8 us; the launch traced here: 94.1 us
  matrix products  20.5 us (22%)
  blocking collectives  18.2 us (19%)
  other arithmetic  17.2 us (18%)
  starting transfers between devices  14.5 us (15%)
  waiting for transfers between devices  10.2 us (11%)
  local copies, waits for them, and re-layouts  9.14 us (10%)
  between operations  4.41 us (5%)
    dot_general x6, matrix products, conv_band(): jnp.einsum('rwk,kf->rwf', stacked[row_shift:row_shift + band_rows], folde...  13.2 us
    all_to_all x1, blocking collectives, local(): lax.all_to_all(flattened, 'step', split_axis=1, concat_axis=0, tiled=True)  12 us
    all_to_all x1, waiting for transfers between devices, local(): lax.all_to_all(running, 'step', split_axis=0, concat_axis=1, tiled=True)  6.58 us
    ppermute x1, starting transfers between devices, from_behind(): return lax.ppermute(x, axis, pairs)  4.85 us
    unnamed x17, local copies, waits for them, and re-layouts  3.95 us
    all_to_all x1, blocking collectives, local(): lax.all_to_all(jnp.stack([key_feats] * lax.axis_size('rows')), 'rows', 0, 0)  3.94 us
    ppermute x2, waiting for transfers between devices, with_halo(): after = lax.ppermute(leading, axis, down)  3.6 us
    ppermute x2, starting transfers between devices, with_halo(): before = lax.ppermute(last, axis, up)  3.53 us
  transfers between devices with their start and end apart: 6, of which 3 were waited for; matrix products, arithmetic and copies ran while one was open for 5% of the time, Pallas kernels for 0%

profile of v1, /device:TPU:0, one launch (start us, length us, event | category | flops | bytes accessed | tf_op | source)
XLA Modules:
  0.0 94.1 jit_solution(10377423351612835618)
XLA Ops:
  0.6 1.0 %copy.34 = f32[1,4,16,512]{3,1,2,0:T(4,128)S(1)} copy(f32[1,4,16,512]{3,2,1,0:T(8,128)} %param.11) | data formatting | bytes 262144 | tf_op args[0]
  1.7 4.8 %collective-permute-start = (f32[1,4,16,512]{3,1,2,0:T(4,128)S(1)}, f32[1,4,16,512]{3,1,2,0:T(4,128)S(1)}, u32[]{:S(2)}, u32[]{:S(2)}) collective-permute-start(f32[1,4,16,512]{3,1,2,0:T(4,128)S(1)} %copy.34), channel_id=1, source_target_pairs={{0,2},{2,4},{4,6},{6,8},{8,10},{10,12},{12,14},{1,3},{3,5},{5,7},{... | collective-permute-start | bytes 393224 | tf_op jit(solution)/shard_map/ppermute | solution.py:14
  6.5 0.7 exponential_multiply_fusion
  7.2 0.6 fusion.43
  9.2 1.0 %copy.36 = bf16[12,16,512]{2,0,1:T(8,128)(2,1)S(1)} copy(bf16[12,16,512]{2,1,0:T(8,128)(2,1)} %param.13) | data formatting | bytes 393216 | tf_op args[2]
  12.2 1.5 %convolution_bitcast_fusion.1 = f32[128]{0:T(128)S(1)} fusion(bf16[17,128]{1,0:T(8,128)(2,1)} %param.15, s32[]{:T(128)} %bitcast.112), kind=kOutput, calls=%fused_computation.34 | convolution fusion | flops 4369 | bytes 4868 | tf_op jit(solution)/shard_map/dot_general | solution.py:97
  13.6 1.0 %multiply_convert_fusion.7 = (bf16[4,16,512]{2,0,1:T(4,128)(2,1)S(1)}, f32[4,16,512]{2,0,1:T(4,128)S(1)}) fusion(f32[]{:T(128)S(6)} %rsqrt.37, f32[1,4,16,512]{3,1,2,0:T(4,128)S(1)} %collective-permute-done, f32[4,16,512]{2,1,0:T(8,128)} %param.12, pred[]{:T(512)S(6)} %eq.11), kind=kLoop, calls=%fused_computation.54 | loop fusion | flops 98304 | bytes 458757 | tf_op jit(solution)/shard_map/convert_element_type | solution.py:95
  14.7 2.6 %fusion.7 = (f32[16,512]{1,0:T(8,128)S(1)}, bf16[16,512,128]{2,1,0:T(8,128)(2,1)S(1)}) fusion(f32[128]{0:T(128)S(1)} %convolution_bitcast_fusion.1, bf16[16,128]{1,0:T(8,128)(2,1)} %param.16, bf16[12,16,512]{2,0,1:T(8,128)(2,1)S(1)} %copy.36, bf16[4,16,512]{2,0,1:T(4,128)(2,1)S(1)} %get-tuple-element.12), kind=kOutput, calls=%fused_computation.14 | convolution fusion | flops 39313408 | bytes 2396672 | tf_op jit(solution)/shard_map/crw,cf->rwf/dot_general | solution.py:99
  17.3 1.5 %fusion.6 = bf16[16,512,128]{2,1,0:T(8,128)(2,1)S(1)} fusion(bf16[16,512,128]{2,1,0:T(8,128)(2,1)S(1)} %get-tuple-element.35, f32[16,512]{1,0:T(8,128)S(1)} %add_rsqrt_fusion.2), kind=kLoop, calls=%fused_computation.13 | loop fusion | flops 7340032 | bytes 4227072 | tf_op jit(solution)/shard_map/convert_element_type | solution.py:40
  18.8 1.5 %collective-permute-start.1 = (bf16[1,512,128]{2,1,0:T(8,128)(2,1)S(1)}, bf16[1,512,128]{2,1,0:T(8,128)(2,1)S(1)}, u32[]{:S(2)}, u32[]{:S(2)}) collective-permute-start(bf16[1,512,128]{2,1,0:T(8,128)(2,1)S(1)} %get-tuple-element.20), channel_id=1, source_target_pairs={{0,1},{2,3},{4,5},{6,7},{8,9},{10,11},{12,13},{14,15},{16,17},{18,... | collective-permute-start | bytes 393224 | tf_op jit(solution)/shard_map/ppermute | solution.py:24
  20.3 1.3 %collective-permute-start.2 = (bf16[1,512,128]{2,1,0:T(8,128)(2,1)S(1)}, bf16[1,512,128]{2,1,0:T(8,128)(2,1)S(1)}, u32[]{:S(2)}, u32[]{:S(2)}) collective-permute-start(bf16[1,512,128]{2,1,0:T(8,128)(2,1)S(1)} %get-tuple-element.21), channel_id=1, source_target_pairs={{1,0},{3,2},{5,4},{7,6},{9,8},{11,10},{13,12},{15,14},{17,16},{19,... | collective-permute-start | bytes 393224 | tf_op jit(solution)/shard_map/ppermute | solution.py:25
  21.7 1.9 %collective-permute-done.2 = bf16[1,512,128]{2,1,0:T(8,128)(2,1)S(1)} collective-permute-done((bf16[1,512,128]{2,1,0:T(8,128)(2,1)S(1)}, bf16[1,512,128]{2,1,0:T(8,128)(2,1)S(1)}, u32[]{:S(2)}, u32[]{:S(2)}) %collective-permute-start.2) | collective-permute-done | bytes 131104 | tf_op jit(solution)/shard_map/ppermute | solution.py:25
  23.6 1.4 %fusion.12 = bf16[18,514,128]{2,1,0:T(8,128)(2,1)S(1)} fusion(bf16[1,512,128]{2,1,0:T(8,128)(2,1)S(1)} %collective-permute-done.2, bf16[16,512,128]{2,1,0:T(8,128)(2,1)S(1)} %fusion.6, bf16[1,512,128]{2,1,0:T(8,128)(2,1)S(1)} %collective-permute-done.1), kind=kLoop, calls=%fused_computation.27 | loop fusion | flops 14211072 | bytes 4727808 | tf_op jit(solution)/shard_map/concatenate | solution.py:26
  25.0 1.4 %fusion.38 = (bf16[18,512,128]{2,1,0:T(8,128)(2,1)S(1)}, bf16[18,512,128]{2,1,0:T(8,128)(2,1)S(1)}) fusion(bf16[18,514,128]{2,1,0:T(8,128)(2,1)S(1)} %fusion.12), kind=kLoop, calls=%fused_computation.73 | loop fusion | bytes 9437184 | tf_op jit(solution)/shard_map/slice | solution.py:53
  26.5 1.1 %pad_maximum_fusion = bf16[18,512,384]{2,1,0:T(8,128)(2,1)S(1)} fusion(bf16[18,512,128]{2,1,0:T(8,128)(2,1)S(1)} %get-tuple-element.17, bf16[1,512,128]{2,1,0:T(8,128)(2,1)S(1)} %collective-permute-done.2, bf16[16,512,128]{2,1,0:T(8,128)(2,1)S(1)} %fusion.6, bf16[1,512,128]{2,1,0:T(8,128)(2,1)S(1)} %collective-permute-done.1, ...), kind=kLoop, calls=%fused_computation.2 | loop fusion | flops 35389440 | bytes 14155776 | tf_op jit(solution)/shard_map/concatenate | solution.py:51
  27.6 1.8 %fusion.47 = f32[16,512,128]{2,1,0:T(8,128)S(1)} fusion(bf16[18,512,384]{2,1,0:T(8,128)(2,1)S(1)} %pad_maximum_fusion, bf16[384,128,1]{1,0,2:T(8,128)(2,1)S(1)} %bitcast.108), kind=kOutput, calls=%fused_computation.82 | convolution fusion | flops 805306368 | bytes 11370496 | tf_op jit(solution)/shard_map/rwk,kf->rwf/dot_general | solution.py:62
  29.4 1.8 %fusion.48 = f32[16,512,128]{2,1,0:T(8,128)S(1)} fusion(bf16[18,512,384]{2,1,0:T(8,128)(2,1)S(1)} %pad_maximum_fusion, bf16[384,128,1]{1,0,2:T(8,128)(2,1)S(1)} %bitcast.106), kind=kOutput, calls=%fused_computation.83 | convolution fusion | flops 805306368 | bytes 11370496 | tf_op jit(solution)/shard_map/rwk,kf->rwf/dot_general | solution.py:62
  31.2 2.1 %multiply_reduce_fusion.1 = (f32[16,512]{1,0:T(8,128)S(1)}, f32[16,512,128]{2,1,0:T(8,128)S(1)}) fusion(bf16[18,512,384]{2,1,0:T(8,128)(2,1)S(1)} %pad_maximum_fusion, bf16[384,128,1]{1,0,2:T(8,128)(2,1)S(1)} %bitcast.104, f32[16,512,128]{2,1,0:T(8,128)S(1)} %fusion.47, f32[16,512,128]{2,1,0:T(8,128)S(1)} %fusion.48), kind=kOutput, calls=%fused_computation.18 | convolution fusion | flops 809492480 | bytes 19791872 | tf_op jit(solution)/shard_map/rwk,kf->rwf/dot_general | solution.py:62
  33.3 1.4 %multiply_convert_fusion.1 = bf16[16,512,128]{2,1,0:T(8,128)(2,1)S(1)} fusion(f32[16,512,128]{2,1,0:T(8,128)S(1)} %get-tuple-element.37, f32[16,512]{1,0:T(8,128)S(1)} %add_rsqrt_fusion.1), kind=kLoop, calls=%fused_computation.17 | loop fusion | flops 6291456 | bytes 6324224 | tf_op jit(solution)/shard_map/convert_element_type | solution.py:40
  34.8 2.1 %collective-permute-start.3 = (bf16[1,512,128]{2,1,0:T(8,128)(2,1)S(1)}, bf16[1,512,128]{2,1,0:T(8,128)(2,1)S(1)}, u32[]{:S(2)}, u32[]{:S(2)}) collective-permute-start(bf16[1,512,128]{2,1,0:T(8,128)(2,1)S(1)} %get-tuple-element.18), channel_id=1, source_target_pairs={{0,1},{2,3},{4,5},{6,7},{8,9},{10,11},{12,13},{14,15},{16,17},{18,... | collective-permute-start | bytes 393224 | tf_op jit(solution)/shard_map/ppermute | solution.py:24
  36.9 1.5 %collective-permute-start.4 = (bf16[1,512,128]{2,1,0:T(8,128)(2,1)S(1)}, bf16[1,512,128]{2,1,0:T(8,128)(2,1)S(1)}, u32[]{:S(2)}, u32[]{:S(2)}) collective-permute-start(bf16[1,512,128]{2,1,0:T(8,128)(2,1)S(1)} %get-tuple-element.19), channel_id=1, source_target_pairs={{1,0},{3,2},{5,4},{7,6},{9,8},{11,10},{13,12},{15,14},{17,16},{19,... | collective-permute-start | bytes 393224 | tf_op jit(solution)/shard_map/ppermute | solution.py:25
  38.4 1.7 %collective-permute-done.4 = bf16[1,512,128]{2,1,0:T(8,128)(2,1)S(1)} collective-permute-done((bf16[1,512,128]{2,1,0:T(8,128)(2,1)S(1)}, bf16[1,512,128]{2,1,0:T(8,128)(2,1)S(1)}, u32[]{:S(2)}, u32[]{:S(2)}) %collective-permute-start.4) | collective-permute-done | bytes 131104 | tf_op jit(solution)/shard_map/ppermute | solution.py:25
  40.1 1.4 %select_maximum_fusion = bf16[18,514,128]{2,1,0:T(8,128)(2,1)S(1)} fusion(bf16[1,512,128]{2,1,0:T(8,128)(2,1)S(1)} %collective-permute-done.4, bf16[16,512,128]{2,1,0:T(8,128)(2,1)S(1)} %multiply_convert_fusion.1, bf16[1,512,128]{2,1,0:T(8,128)(2,1)S(1)} %collective-permute-done.3), kind=kLoop, calls=%fused_computation.21 | loop fusion | flops 14211072 | bytes 4727808 | tf_op jit(solution)/shard_map/concatenate | solution.py:26
  41.6 1.5 %fusion.37 = (bf16[18,512,128]{2,1,0:T(8,128)(2,1)S(1)}, bf16[18,512,128]{2,1,0:T(8,128)(2,1)S(1)}) fusion(bf16[18,514,128]{2,1,0:T(8,128)(2,1)S(1)} %select_maximum_fusion), kind=kLoop, calls=%fused_computation.72 | loop fusion | bytes 9437184 | tf_op jit(solution)/shard_map/slice | solution.py:53
  43.0 1.1 %pad_maximum_fusion.1 = bf16[18,512,384]{2,1,0:T(8,128)(2,1)S(1)} fusion(bf16[18,512,128]{2,1,0:T(8,128)(2,1)S(1)} %get-tuple-element.15, bf16[1,512,128]{2,1,0:T(8,128)(2,1)S(1)} %collective-permute-done.4, bf16[16,512,128]{2,1,0:T(8,128)(2,1)S(1)} %multiply_convert_fusion.1, bf16[1,512,128]{2,1,0:T(8,128)(2,1)S(1)} %collective-permute-done.3, ...), kind=kLoop, calls=%fused_computation.3 | loop fusion | flops 35389440 | bytes 14155776 | tf_op jit(solution)/shard_map/concatenate | solution.py:51
  44.2 1.8 %fusion.49 = f32[16,512,128]{2,1,0:T(8,128)S(1)} fusion(bf16[18,512,384]{2,1,0:T(8,128)(2,1)S(1)} %pad_maximum_fusion.1, bf16[384,128,1]{1,0,2:T(8,128)(2,1)S(1)} %bitcast.109), kind=kOutput, calls=%fused_computation.84 | convolution fusion | flops 805306368 | bytes 11370496 | tf_op jit(solution)/shard_map/rwk,kf->rwf/dot_general | solution.py:62
  46.0 1.8 %fusion.50 = f32[16,512,128]{2,1,0:T(8,128)S(1)} fusion(bf16[18,512,384]{2,1,0:T(8,128)(2,1)S(1)} %pad_maximum_fusion.1, bf16[384,128,1]{1,0,2:T(8,128)(2,1)S(1)} %bitcast.107), kind=kOutput, calls=%fused_computation.85 | convolution fusion | flops 805306368 | bytes 11370496 | tf_op jit(solution)/shard_map/rwk,kf->rwf/dot_general | solution.py:62
  47.8 3.9 %convert_add_fusion = f32[16,512,128]{2,1,0:T(8,128)} fusion(bf16[16,512,128]{2,1,0:T(8,128)(2,1)S(1)} %get-tuple-element.35, f32[16,512,128]{2,1,0:T(8,128)S(1)} %fusion.49, f32[16,512,128]{2,1,0:T(8,128)S(1)} %fusion.50, bf16[18,512,384]{2,1,0:T(8,128)(2,1)S(1)} %pad_maximum_fusion.1, bf16[384,128,1]{1,0,2:T(8,128)(2,1)S(1)} %bitcast.105), kind=kOutput, calls=%fused_computation.4 | convolution fusion | flops 809500672 | bytes 21856256 | tf_op jit(solution)/shard_map/rwk,kf->rwf/dot_general | solution.py:62
  51.7 3.2 %reduce_sum.60 = f32[4,128,128]{2,1,0:T(8,128)S(1)} reduce(f32[4,4,128,4,128]{4,3,2,1,0:T(4,128)} %bitcast.99, f32[]{:T(128)} %constant.40.clone.1), dimensions={1,3}, to_apply=%region_2.3 | reduce | flops 983040 | bytes 4456452 | tf_op jit(solution)/shard_map/reduce_sum | solution.py:114
  55.2 0.3 fusion.44
  55.7 3.9 %all_to_all.29 = bf16[2,512,128]{1,2,0:T(8,128)(2,1)S(1)} all-to-all(bf16[2,512,128]{1,2,0:T(8,128)(2,1)S(1)} %pad_maximum_fusion.2), channel_id=1, replica_groups=mesh['ens'=2,'step'=8,'rows'=2] {'rows'}, dimensions={0} | all-to-all | bytes 524288 | tf_op jit(solution)/shard_map/all_to_all | solution.py:123
  59.9 0.2 fusion.46
  60.1 0.3 copy.37
  60.6 2.2 %all_gather.3 = bf16[1024,128]{0,1:T(8,128)(2,1)S(1)} all-gather(bf16[512,128]{0,1:T(8,128)(2,1)S(1)} %slice.132), channel_id=1, replica_groups=mesh['ens'=2,'step'=8,'rows'=2] {'rows'}, dimensions={0}, use_global_device_ids=true | all-gather | bytes 393216 | tf_op jit(solution)/shard_map/all_gather | solution.py:125
  62.8 0.2 fusion.45
  63.0 0.4 fusion.15
  63.7 0.8 broadcast_in_dim.6
  64.5 1.1 %copy-done.1 = f32[16,512,128]{2,1,0:T(8,128)S(1)} copy-done((f32[16,512,128]{2,1,0:T(8,128)S(1)}, f32[16,512,128]{2,1,0:T(8,128)}, u32[]{:S(2)}) %copy-start.1) | copy-done | bytes 4194328
  65.6 1.2 %multiply_reduce_fusion = (f32[16,512]{1,0:T(8,128)S(1)}, f32[16,512,128]{2,1,0:T(8,128)S(1)}) fusion(f32[16,512,128]{2,1,0:T(8,128)S(1)} %copy-done.1, f32[16,512,128]{2,1,0:T(8,128)S(1)} %bitcast.100), kind=kLoop, calls=%fused_computation.16 | loop fusion | flops 3137536 | bytes 12615680 | tf_op jit(solution)/shard_map/reduce_sum | solution.py:36
  66.8 1.9 %fusion.17 = f32[4,16,512]{2,0,1:T(4,128)S(1)} fusion(f32[16,512,128]{2,1,0:T(8,128)S(1)} %get-tuple-element.11, f32[16,512]{1,0:T(8,128)S(1)} %add_rsqrt_fusion, f32[]{:T(128)S(6)} %mul.111, bf16[128,4]{0,1:T(4,128)(2,1)S(1)} %copy-done.6), kind=kOutput, calls=%fused_computation.33 | convolution fusion | flops 14712832 | bytes 4359172 | tf_op jit(solution)/shard_map/rwf,fc->crw/dot_general | solution.py:142
  68.7 0.7 fusion.27
  69.7 12.0 %all_to_all.30 = f32[1,8,4096]{2,0,1:T(1,128)S(1)} all-to-all(f32[1,8,4096]{2,0,1:T(1,128)S(1)} %all_to_all.25), channel_id=1, replica_groups=mesh['ens'=2,'step'=8,'rows'=2] {'step'}, dimensions={1} | all-to-all | bytes 262144 | tf_op jit(solution)/shard_map/all_to_all | solution.py:148
  81.7 0.7 fusion.23
  82.4 3.4 %all-to-all-start.2 = ((f32[8,1,4096]{2,1,0:T(1,128)}), f32[8,1,4096]{2,1,0:T(1,128)S(1)}, u32[]{:S(2)}, u32[]{:S(2)}) async-start(f32[8,1,4096]{2,1,0:T(1,128)} %fusion.23), calls=%async_computation.2 | async-start | bytes 262144 | tf_op jit(solution)/shard_map/all_to_all | solution.py:150
  85.8 0.7 copy.42
  86.5 6.6 %all-to-all-done.2 = f32[8,1,4096]{2,1,0:T(1,128)S(1)} async-done(((f32[8,1,4096]{2,1,0:T(1,128)}), f32[8,1,4096]{2,1,0:T(1,128)S(1)}, u32[]{:S(2)}, u32[]{:S(2)}) %all-to-all-start.2) | async-done | bytes 131104 | tf_op jit(solution)/shard_map/all_to_all | solution.py:150
  93.1 0.3 reduce.2
  93.4 0.7 add_bitcast_fusion
  (38 shorter events, 1.5 us)
Async XLA Ops:
  0.6 54.6 %copy-start = (bf16[128,384]{1,0:T(8,128)(2,1)S(1)}, bf16[128,384]{1,0:T(8,128)(2,1)}, u32[]{:S(2)}) copy-start(bf16[128,384]{1,0:T(8,128)(2,1)} %param.19) | copy-start | bytes 294916
  1.7 12.0 %collective-permute-start = (f32[1,4,16,512]{3,1,2,0:T(4,128)S(1)}, f32[1,4,16,512]{3,1,2,0:T(4,128)S(1)}, u32[]{:S(2)}, u32[]{:S(2)}) collective-permute-start(f32[1,4,16,512]{3,1,2,0:T(4,128)S(1)} %copy.34), channel_id=1, source_target_pairs={{0,2},{2,4},{4,6},{6,8},{8,10},{10,12},{12,14},{1,3},{3,5},{5,7},{... | collective-permute-start | bytes 393224 | tf_op jit(solution)/shard_map/ppermute | solution.py:14
  14.7 7.0 %copy-start.3 = (bf16[3,3,128,128]{3,2,1,0:T(8,128)(2,1)S(1)}, bf16[3,3,128,128]{3,2,1,0:T(8,128)(2,1)}, u32[]{:S(2)}) copy-start(bf16[3,3,128,128]{3,2,1,0:T(8,128)(2,1)} %param.17) | copy-start | bytes 884740
  18.8 2.8 %collective-permute-start.1 = (bf16[1,512,128]{2,1,0:T(8,128)(2,1)S(1)}, bf16[1,512,128]{2,1,0:T(8,128)(2,1)S(1)}, u32[]{:S(2)}, u32[]{:S(2)}) collective-permute-start(bf16[1,512,128]{2,1,0:T(8,128)(2,1)S(1)} %get-tuple-element.20), channel_id=1, source_target_pairs={{0,1},{2,3},{4,5},{6,7},{8,9},{10,11},{12,13},{14,15},{16,17},{18,... | collective-permute-start | bytes 393224 | tf_op jit(solution)/shard_map/ppermute | solution.py:24
  20.3 3.2 %collective-permute-start.2 = (bf16[1,512,128]{2,1,0:T(8,128)(2,1)S(1)}, bf16[1,512,128]{2,1,0:T(8,128)(2,1)S(1)}, u32[]{:S(2)}, u32[]{:S(2)}) collective-permute-start(bf16[1,512,128]{2,1,0:T(8,128)(2,1)S(1)} %get-tuple-element.21), channel_id=1, source_target_pairs={{1,0},{3,2},{5,4},{7,6},{9,8},{11,10},{13,12},{15,14},{17,16},{19,... | collective-permute-start | bytes 393224 | tf_op jit(solution)/shard_map/ppermute | solution.py:25
  33.3 5.1 %copy-start.4 = (bf16[3,3,128,128]{3,2,1,0:T(8,128)(2,1)S(1)}, bf16[3,3,128,128]{3,2,1,0:T(8,128)(2,1)}, u32[]{:S(2)}) copy-start(bf16[3,3,128,128]{3,2,1,0:T(8,128)(2,1)} %param.18) | copy-start | bytes 884740
  34.8 3.6 %collective-permute-start.3 = (bf16[1,512,128]{2,1,0:T(8,128)(2,1)S(1)}, bf16[1,512,128]{2,1,0:T(8,128)(2,1)S(1)}, u32[]{:S(2)}, u32[]{:S(2)}) collective-permute-start(bf16[1,512,128]{2,1,0:T(8,128)(2,1)S(1)} %get-tuple-element.18), channel_id=1, source_target_pairs={{0,1},{2,3},{4,5},{6,7},{8,9},{10,11},{12,13},{14,15},{16,17},{18,... | collective-permute-start | bytes 393224 | tf_op jit(solution)/shard_map/ppermute | solution.py:24
  36.9 3.2 %collective-permute-start.4 = (bf16[1,512,128]{2,1,0:T(8,128)(2,1)S(1)}, bf16[1,512,128]{2,1,0:T(8,128)(2,1)S(1)}, u32[]{:S(2)}, u32[]{:S(2)}) collective-permute-start(bf16[1,512,128]{2,1,0:T(8,128)(2,1)S(1)} %get-tuple-element.19), channel_id=1, source_target_pairs={{1,0},{3,2},{5,4},{7,6},{9,8},{11,10},{13,12},{15,14},{17,16},{19,... | collective-permute-start | bytes 393224 | tf_op jit(solution)/shard_map/ppermute | solution.py:25
  54.9 8.5 %copy-start.5 = (bf16[128,128]{1,0:T(8,128)(2,1)S(1)}, bf16[128,128]{1,0:T(8,128)(2,1)}, u32[]{:S(2)}) copy-start(bf16[128,128]{1,0:T(8,128)(2,1)} %param.20) | copy-start | bytes 98308
  63.4 2.2 %copy-start.1 = (f32[16,512,128]{2,1,0:T(8,128)S(1)}, f32[16,512,128]{2,1,0:T(8,128)}, u32[]{:S(2)}) copy-start(f32[16,512,128]{2,1,0:T(8,128)} %convert_add_fusion) | copy-start | bytes 12582916
  65.6 1.2 %copy-start.6 = (bf16[128,4]{0,1:T(4,128)(2,1)S(1)}, bf16[128,4]{0,1:T(4,128)(2,1)}, u32[]{:S(2)}) copy-start(bf16[128,4]{0,1:T(4,128)(2,1)} %param.21) | copy-start | bytes 3076
  66.8 26.6 %copy-start.2 = (f32[4,16,512]{2,1,0:T(8,128)S(1)}, f32[4,16,512]{2,1,0:T(8,128)}, u32[]{:S(2)}) copy-start(f32[4,16,512]{2,1,0:T(8,128)} %param.12) | copy-start | bytes 393220
  82.4 10.7 %all-to-all-start.2 = ((f32[8,1,4096]{2,1,0:T(1,128)}), f32[8,1,4096]{2,1,0:T(1,128)S(1)}, u32[]{:S(2)}, u32[]{:S(2)}) async-start(f32[8,1,4096]{2,1,0:T(1,128)} %fusion.23), calls=%async_computation.2 | async-start | bytes 262144 | tf_op jit(solution)/shard_map/all_to_all | solution.py:150
